TPU v7x, 512 devices: a whole 4x4x16 slice. The times are simulated.
512 devices in a mesh: section: 32 (over z, core), blk: 16 (over y, x).
Axes of the slice: x: 4, y: 4, z: 16, core: 2. Of those that a mesh axis runs over, the one named last changes fastest.
Arguments:
- held_input: bfloat16 [32, 5120, 128], P('section', 'blk'), may hold values from -6 to 6
- fresh_input: bfloat16 [5120, 128], P('blk'), may hold values from -6 to 6
- stashed: bfloat16 [32, 2, 5120, 128], P('section', None, 'blk'), may hold values from -6 to 6
- held_grad: bfloat16 [32, 5120, 128], P('section', 'blk'), may hold values from -6 to 6
- fresh_grad: bfloat16 [5120, 128], P('blk'), may hold values from -6 to 6
- first_up: bfloat16 [32, 2, 128, 6400], P('section', None, 'blk'), may hold values from -1 to 1
- second_up: bfloat16 [32, 2, 160, 16384], P('section', None, 'blk'), may hold values from -0.5 to 0.5
- first_down: bfloat16 [32, 160, 16384], P('section', 'blk'), may hold values from -0.5 to 0.5
- second_down: bfloat16 [32, 128, 6400], P('section', 'blk'), may hold values from -0.5 to 0.5
Outputs:
- passed_output: bfloat16 [32, 5120, 128], P('section', 'blk')
- passed_grad: bfloat16 [32, 5120, 128], P('section', 'blk')
- grad_first_up: bfloat16 [32, 2, 128, 6400], P('section', None, 'blk')
- grad_second_up: bfloat16 [32, 2, 160, 16384], P('section', None, 'blk')
- grad_first_down: bfloat16 [32, 160, 16384], P('section', 'blk')
- grad_second_down: bfloat16 [32, 128, 6400], P('section', 'blk')
All inputs are finite; a program needn't handle non-finite values.
Results may differ from a plain program's by a relative error of at most 0.0095.
Values may be sent and summed in bfloat16 or wider, within the bound.
No kernel may reach another device: no remote copies, remote signals or barrier semaphores. Data moves between devices by JAX's collectives and lax.ppermute only.
A program may use at most 64 MiB of HBM per device.

v0:
```python
import math
import jax
import jax.numpy as jnp
from jax import lax
from jax.sharding import PartitionSpec as P

BLOCK = 128
FIRST_BLOCKS = 128
FIRST_IN = 40
SECOND_BLOCKS = 160
TICKS = 2


def from_behind(value, axis, by):
    length = lax.axis_size(axis)
    pairs = [(i, i + by) for i in range(length) if 0 <= i + by < length]
    return lax.ppermute(value, axis, pairs)


def to_blocks(pieces):
    return lax.all_to_all(pieces, "blk", split_axis=1, concat_axis=0, tiled=True)


def to_features(pieces):
    groups = lax.axis_size("blk")
    r_local, p_all, n = pieces.shape
    p_local = p_all // groups
    grouped = pieces.reshape(r_local, groups, p_local, n).transpose(1, 0, 2, 3)
    arrived = lax.all_to_all(grouped, "blk", split_axis=0, concat_axis=0, tiled=True)
    return arrived.reshape(groups * r_local, p_local, n)


def spread_of(values, up_first):
    return jnp.einsum(
        "pqt,gpqr->prgt", values, up_first, preferred_element_type=jnp.float32
    ).astype(jnp.bfloat16)


def lowered_grad_of(grads, down_second):
    return jnp.einsum(
        "pqt,prq->prt", grads, down_second, preferred_element_type=jnp.float32
    ).astype(jnp.bfloat16)


def forward_middle(spread_r, up_second, down_first):
    mixed = jnp.einsum("prgt,grpo->grot", spread_r, up_second, preferred_element_type=jnp.float32)
    hidden = (jax.nn.silu(mixed[0]) * mixed[1]).astype(jnp.bfloat16)
    lowered = jnp.einsum(
        "rot,rop->rpt", hidden, down_first, preferred_element_type=jnp.float32
    ).astype(jnp.bfloat16)
    return (mixed, hidden, lowered)


def backward_middle(mixed, grad_lowered_r, up_second, down_first):
    grad_hidden = jnp.einsum(
        "prt,rop->rot", grad_lowered_r, down_first, preferred_element_type=jnp.float32
    )
    sigmoid_gate = jax.nn.sigmoid(mixed[0])
    slope = sigmoid_gate * (1.0 + mixed[0] * (1.0 - sigmoid_gate))
    grad_mixed = jnp.stack(
        [grad_hidden * mixed[1] * slope, grad_hidden * mixed[0] * sigmoid_gate]
    ).astype(jnp.bfloat16)
    grad_spread = jnp.einsum(
        "grot,grpo->grpt", grad_mixed, up_second, preferred_element_type=jnp.float32
    ).astype(jnp.bfloat16)
    return (grad_mixed, grad_spread)


def output_of(values, lowered_p, down_second):
    added = jnp.einsum("rpt,prq->pqt", lowered_p, down_second, preferred_element_type=jnp.float32)
    return (values.astype(jnp.float32) + added).astype(jnp.bfloat16)


def input_grad_of(grads, grad_spread_p, up_first):
    added = jnp.einsum(
        "rpgt,gpqr->pqt", grad_spread_p, up_first, preferred_element_type=jnp.float32
    )
    return (grads.astype(jnp.float32) + added).astype(jnp.bfloat16)


def shards(
    held_input,
    fresh_input,
    stashed,
    held_grad,
    fresh_grad,
    first_up,
    second_up,
    first_down,
    second_down,
):
    feature_blocks = first_up.shape[2]
    hidden_blocks = second_up.shape[2]
    tokens = held_input.shape[2]
    up_first = first_up[0].reshape(2, feature_blocks, FIRST_IN, SECOND_BLOCKS)
    up_second = second_up[0].reshape(2, hidden_blocks, FIRST_BLOCKS, BLOCK)
    down_first = first_down[0].reshape(hidden_blocks, BLOCK, FIRST_BLOCKS)
    down_second = second_down[0].reshape(feature_blocks, SECOND_BLOCKS, FIRST_IN)
    first_inputs = held_input[0].reshape(feature_blocks, FIRST_IN, tokens)
    first_grads = held_grad[0].reshape(feature_blocks, FIRST_IN, tokens)
    stash_views = [stashed[0, k].reshape(feature_blocks, FIRST_IN, tokens) for k in range(TICKS)]
    section_pos = lax.axis_index("section")
    last_section = lax.axis_size("section") - 1
    t = tokens
    values_a = jnp.concatenate([first_inputs] + stash_views, axis=2)
    spread_a = spread_of(values_a, up_first)
    glow_1 = lowered_grad_of(first_grads, down_second)
    payload = jnp.concatenate(
        [spread_a.reshape(feature_blocks, SECOND_BLOCKS, 2 * 3 * t), glow_1], axis=2
    )
    arrived = to_blocks(payload)
    spread_ar = arrived[:, :, : 6 * t].reshape(FIRST_BLOCKS, hidden_blocks, 2, 3 * t)
    glow_1r = arrived[:, :, 6 * t :]
    mixed_a, hidden_a, lowered_a = forward_middle(spread_ar, up_second, down_first)
    gmix_1, gspread_1 = backward_middle(mixed_a[:, :, :, t : 2 * t], glow_1r, up_second, down_first)
    payload = jnp.concatenate([lowered_a, gspread_1[0], gspread_1[1]], axis=2)
    back = to_features(payload)
    lowered_ap = back[:, :, : 3 * t]
    gspread_1p = back[:, :, 3 * t :].reshape(SECOND_BLOCKS, feature_blocks, 2, t)
    outputs = output_of(first_inputs, lowered_ap[:, :, :t], down_second)
    backward = input_grad_of(first_grads, gspread_1p, up_first)
    moved_forward = from_behind(outputs, "section", 1)
    inputs = jnp.where(
        section_pos == 0, fresh_input.reshape(feature_blocks, FIRST_IN, tokens), moved_forward
    )
    moved_backward = from_behind(backward, "section", -1)
    grads = jnp.where(
        section_pos == last_section,
        fresh_grad.reshape(feature_blocks, FIRST_IN, tokens),
        moved_backward,
    )
    spread_b = spread_of(inputs, up_first)
    glow_2 = lowered_grad_of(grads, down_second)
    payload = jnp.concatenate(
        [spread_b.reshape(feature_blocks, SECOND_BLOCKS, 2 * t), glow_2], axis=2
    )
    arrived = to_blocks(payload)
    spread_br = arrived[:, :, : 2 * t].reshape(FIRST_BLOCKS, hidden_blocks, 2, t)
    glow_2r = arrived[:, :, 2 * t :]
    _, _, lowered_b = forward_middle(spread_br, up_second, down_first)
    gmix_2, gspread_2 = backward_middle(mixed_a[:, :, :, 2 * t :], glow_2r, up_second, down_first)
    payload = jnp.concatenate([lowered_b, gspread_2[0], gspread_2[1]], axis=2)
    back = to_features(payload)
    lowered_bp = back[:, :, :t]
    gspread_2p = back[:, :, t:].reshape(SECOND_BLOCKS, feature_blocks, 2, t)
    outputs = output_of(inputs, lowered_bp, down_second)
    backward = input_grad_of(grads, gspread_2p, up_first)
    stash_both = jnp.concatenate(stash_views, axis=2)
    gspread_both = jnp.concatenate([gspread_1p, gspread_2p], axis=3)
    spread_both = spread_ar[:, :, :, t:]
    gmix_both = jnp.concatenate([gmix_1, gmix_2], axis=3)
    hidden_both = hidden_a[:, :, t:]
    glow_both = jnp.concatenate([glow_1r, glow_2r], axis=2)
    lowered_both = lowered_ap[:, :, t:]
    grads_both = jnp.concatenate([first_grads, grads], axis=2)
    total_first_up = jnp.einsum(
        "pqt,rpgt->gpqr", stash_both, gspread_both, preferred_element_type=jnp.float32
    )
    total_second_up = jnp.einsum(
        "prgt,grot->grpo", spread_both, gmix_both, preferred_element_type=jnp.float32
    )
    total_first_down = jnp.einsum(
        "rot,prt->rop", hidden_both, glow_both, preferred_element_type=jnp.float32
    )
    total_second_down = jnp.einsum(
        "rpt,pqt->prq", lowered_both, grads_both, preferred_element_type=jnp.float32
    )
    factor = 1.0 / math.sqrt(TICKS * tokens)
    return (
        outputs.reshape(held_input.shape),
        backward.reshape(held_grad.shape),
        (total_first_up * factor).astype(jnp.bfloat16).reshape(first_up.shape),
        (total_second_up * factor).astype(jnp.bfloat16).reshape(second_up.shape),
        (total_first_down * factor).astype(jnp.bfloat16).reshape(first_down.shape),
        (total_second_down * factor).astype(jnp.bfloat16).reshape(second_down.shape),
    )


def solution(mesh):
    return jax.shard_map(
        shards,
        mesh=mesh,
        in_specs=(
            P("section", "blk", None),
            P("blk", None),
            P("section", None, "blk", None),
            P("section", "blk", None),
            P("blk", None),
            P("section", None, "blk", None),
            P("section", None, "blk", None),
            P("section", "blk", None),
            P("section", "blk", None),
        ),
        out_specs=(
            P("section", "blk", None),
            P("section", "blk", None),
            P("section", None, "blk", None),
            P("section", None, "blk", None),
            P("section", "blk", None),
            P("section", "blk", None),
        ),
        check_vma=False,
    )
```

profile of v0, /device:TPU:224, one launch (start us, length us, event | category | flops | bytes accessed | tf_op | source)
XLA Modules:
  0.0 168.3 jit_solution(5044812806253064722)
XLA Ops:
  0.6 0.9 fusion.103
  1.6 1.4 reshape_squeeze.27
  3.0 1.6 reshape_squeeze.28
  4.5 1.6 convert_bitcast_fusion
  6.4 0.7 copy-done.27
  7.5 2.1 %copy.143 = bf16[8,160,896]{2,0,1:T(8,128)(2,1)} copy(bf16[8,160,896]{2,1,0:T(8,128)(2,1)S(1)} %pad_maximum_fusion) | data formatting | bytes 4587520 | tf_op jit(solution)/shard_map/concatenate | solution.py:108
  9.6 7.2 %all-to-all-start = ((bf16[8,160,896]{2,0,1:T(8,128)(2,1)}), bf16[8,160,896]{2,0,1:T(8,128)(2,1)S(1)}, u32[]{:S(2)}, u32[]{:S(2)}) async-start(bf16[8,160,896]{2,0,1:T(8,128)(2,1)} %copy.143), calls=%async_computation | async-start | bytes 4587520 | tf_op jit(solution)/shard_map/all_to_all | solution.py:21
  16.8 0.9 copy.218
  17.7 2.3 %reshape_squeeze.30 = bf16[2,10,128,128]{3,2,0,1:T(8,128)(2,1)S(1)} reshape(bf16[1,2,10,16384]{3,1,2,0:T(2,128)(2,1)} %param.15) | data formatting | bytes 1310720 | tf_op jit(solution)/shard_map/reshape;squeeze | solution.py:96
  20.0 31.3 %all-to-all-done = bf16[8,160,896]{2,0,1:T(8,128)(2,1)S(1)} async-done(((bf16[8,160,896]{2,0,1:T(8,128)(2,1)}), bf16[8,160,896]{2,0,1:T(8,128)(2,1)S(1)}, u32[]{:S(2)}, u32[]{:S(2)}) %all-to-all-start) | async-done | bytes 2293792 | tf_op jit(solution)/shard_map/all_to_all | solution.py:21
  51.3 1.4 copy-done.1
  52.8 2.0 %copy.262 = bf16[16,8,10,896]{3,1,0,2:T(8,128)(2,1)S(1)} copy(bf16[16,8,10,896]{3,1,2,0:T(8,128)(2,1)} %bitcast.213) | data formatting | bytes 4587520 | tf_op jit(solution)/shard_map/all_to_all | solution.py:21
  54.7 1.5 slice.113
  56.2 4.0 %copy.145 = bf16[128,10,768]{0,2,1:T(8,128)(2,1)} copy(bf16[128,10,768]{2,0,1:T(8,128)(2,1)} %slice.113) | data formatting | bytes 3932160 | tf_op jit(solution)/shard_map/slice | solution.py:112
  60.2 2.2 %convolution_bitcast_fusion = f32[2,10,128,384]{2,3,1,0:T(8,128)S(1)} fusion(bf16[128,10,2,384]{0,3,2,1:T(8,128)(2,1)} %bitcast.214, bf16[2,10,128,128]{3,2,0,1:T(8,128)(2,1)S(1)} %reshape_squeeze.30), kind=kOutput, calls=%fused_computation.2 | convolution fusion | flops 251658240 | bytes 6553600 | tf_op jit(solution)/shard_map/prgt,grpo->grot/dot_general | solution.py:46
  62.9 1.3 copy-done
  66.1 1.4 copy_bitcast_fusion.1
  67.5 4.4 %all-to-all-start.1 = ((bf16[16,10,8,640]{3,2,1,0:T(8,128)(2,1)}), bf16[16,10,8,640]{3,2,1,0:T(8,128)(2,1)}, u32[]{:S(2)}, u32[]{:S(2)}) async-start(bf16[16,10,8,640]{3,2,1,0:T(8,128)(2,1)} %copy_bitcast_fusion.1), calls=%async_computation.1 | async-start | bytes 3276800 | tf_op jit(solution)/shard_map/all_to_all | solution.py:29
  71.9 23.7 %all-to-all-done.1 = bf16[16,10,8,640]{3,2,1,0:T(8,128)(2,1)} async-done(((bf16[16,10,8,640]{3,2,1,0:T(8,128)(2,1)}), bf16[16,10,8,640]{3,2,1,0:T(8,128)(2,1)}, u32[]{:S(2)}, u32[]{:S(2)}) %all-to-all-start.1) | async-done | bytes 1638432 | tf_op jit(solution)/shard_map/all_to_all | solution.py:29
  95.6 1.0 slice.121
  96.7 2.3 %fusion.102 = (bf16[160,8,256]{2,1,0:T(8,128)(2,1)}, bf16[160,8,2,128]{3,1,2,0:T(8,128)(2,1)S(1)}) fusion(bf16[160,8,640]{2,1,0:T(8,128)(2,1)} %bitcast.26), kind=kLoop, calls=%fused_computation.143 | loop fusion | bytes 2621440 | tf_op jit(solution)/shard_map/slice | solution.py:154
  99.0 1.4 fusion.35
  100.3 1.9 %collective-permute-start.1 = (bf16[8,40,128]{2,1,0:T(8,128)(2,1)S(1)}, bf16[8,40,128]{2,1,0:T(8,128)(2,1)S(1)}, u32[]{:S(2)}, u32[]{:S(2)}) collective-permute-start(bf16[8,40,128]{2,1,0:T(8,128)(2,1)S(1)} %fusion.35), channel_id=1, source_target_pairs={{16,0},{32,16},{48,32},{64,48},{80,64},{96,80},{112,96},{128,112},... | collective-permute-start | bytes 245768 | tf_op jit(solution)/shard_map/ppermute | solution.py:17
  102.6 2.4 %collective-permute-start = (bf16[8,40,128]{2,1,0:T(8,128)(2,1)S(1)}, bf16[8,40,128]{2,1,0:T(8,128)(2,1)S(1)}, u32[]{:S(2)}, u32[]{:S(2)}) collective-permute-start(bf16[8,40,128]{2,1,0:T(8,128)(2,1)S(1)} %fusion.36), channel_id=1, source_target_pairs={{0,16},{16,32},{32,48},{48,64},{64,80},{80,96},{96,112},{112,128},... | collective-permute-start | bytes 245768 | tf_op jit(solution)/shard_map/ppermute | solution.py:17
  105.3 3.1 %collective-permute-done = bf16[8,40,128]{2,1,0:T(8,128)(2,1)S(1)} collective-permute-done((bf16[8,40,128]{2,1,0:T(8,128)(2,1)S(1)}, bf16[8,40,128]{2,1,0:T(8,128)(2,1)S(1)}, u32[]{:S(2)}, u32[]{:S(2)}) %collective-permute-start) | collective-permute-done | bytes 81952 | tf_op jit(solution)/shard_map/ppermute | solution.py:17
  109.4 20.6 %all_to_all.46 = bf16[8,160,384]{2,0,1:T(8,128)(2,1)S(1)} all-to-all(bf16[8,160,384]{2,0,1:T(8,128)(2,1)S(1)} %copy.163), channel_id=1, replica_groups=mesh['section'=32,'blk'=16] {'blk'}, dimensions={1} | all-to-all | bytes 1966080 | tf_op jit(solution)/shard_map/all_to_all | solution.py:21
  130.1 2.2 %fusion.67 = (bf16[1,10,128,128]{2,3,1,0:T(8,128)(2,1)S(1)}, bf16[1,10,128,128]{2,3,1,0:T(8,128)(2,1)S(1)}) fusion(f32[2,10,128,384]{2,3,1,0:T(8,128)} %copy-done, bf16[16,128,128]{2,1,0:T(8,128)(2,1)S(1)} %bitcast.225, bf16[128,10,384]{2,0,1:T(8,128)(2,1)S(1)} %bitcast.217), kind=kOutput, calls=%fused_computation.106 | convolution fusion | flops 44072960 | bytes 2621440 | tf_op jit(solution)/shard_map/prt,rop->rot/dot_general | solution.py:55
  132.3 1.0 slice.123
  133.9 0.9 slice_bitcast_fusion.11
  134.8 2.2 %copy.165 = bf16[128,10,256]{0,2,1:T(8,128)(2,1)} copy(bf16[128,10,256]{2,0,1:T(8,128)(2,1)} %slice.123) | data formatting | bytes 1310720 | tf_op jit(solution)/shard_map/slice | solution.py:138
  137.0 1.5 convolution_bitcast_fusion.1
  139.6 1.2 copy_bitcast_fusion.2
  140.7 4.4 %all-to-all-start.3 = ((bf16[16,10,8,384]{3,2,1,0:T(8,128)(2,1)}), bf16[16,10,8,384]{3,2,1,0:T(8,128)(2,1)}, u32[]{:S(2)}, u32[]{:S(2)}) async-start(bf16[16,10,8,384]{3,2,1,0:T(8,128)(2,1)} %copy_bitcast_fusion.2), calls=%async_computation.3 | async-start | bytes 1966080 | tf_op jit(solution)/shard_map/all_to_all | solution.py:29
  145.2 0.8 slice.116
  146.0 1.9 %copy.210 = bf16[128,10,128]{0,2,1:T(8,128)(2,1)} copy(bf16[128,10,128]{2,0,1:T(8,128)(2,1)} %slice.116) | data formatting | bytes 655360
  147.9 1.0 copy.160
  148.9 1.4 fusion.32
  150.6 1.1 reshape.87
  151.7 1.0 slice.126
  152.7 1.7 %fusion.3 = bf16[2,10,128,128]{3,2,1,0:T(8,128)(2,1)S(1)} fusion(bf16[1,10,128,128]{2,3,1,0:T(8,128)(2,1)} %copy-done.33, bf16[1,10,128,128]{2,3,1,0:T(8,128)(2,1)} %copy-done.32, bf16[1,10,128,128]{2,3,1,0:T(8,128)(2,1)} %copy-done.31, bf16[1,10,128,128]{2,3,1,0:T(8,128)(2,1)S(1)} %copy-done.30, bf16[128,10,2,384]{0,3,2,1:T(8,128)(2,1)S(1)} %bitcast.215), kind=kOutput, calls=%fused_computation.14 | convolution fusion | flops 173670400 | bytes 3276800 | tf_op jit(solution)/shard_map/prgt,grot->grpo/dot_general | solution.py:159
  154.5 1.0 reshape.85
  156.3 1.0 reshape.86
  157.3 4.9 %all-to-all-done.3 = bf16[16,10,8,384]{3,2,1,0:T(8,128)(2,1)} async-done(((bf16[16,10,8,384]{3,2,1,0:T(8,128)(2,1)}), bf16[16,10,8,384]{3,2,1,0:T(8,128)(2,1)}, u32[]{:S(2)}, u32[]{:S(2)}) %all-to-all-start.3) | async-done | bytes 983072 | tf_op jit(solution)/shard_map/all_to_all | solution.py:29
  162.2 1.0 slice.131
  163.2 1.3 slice_bitcast_fusion.2
  164.5 1.0 add_convert_fusion
  166.7 0.7 copy.189
  167.4 0.9 add_convert_fusion.1
  (91 shorter events, 8.6 us)
Async XLA Ops:
  2.9 1.6 copy-start.6
  6.2 0.9 copy-start.27
  9.6 7.2 %copy-start.17 = (bf16[1,10,16384]{2,1,0:T(8,128)(2,1)S(1)}, bf16[1,10,16384]{2,1,0:T(8,128)(2,1)}, u32[]{:S(2)}) copy-start(bf16[1,10,16384]{2,1,0:T(8,128)(2,1)} %param.16) | copy-start | bytes 983044
  9.6 41.7 %all-to-all-start = ((bf16[8,160,896]{2,0,1:T(8,128)(2,1)}), bf16[8,160,896]{2,0,1:T(8,128)(2,1)S(1)}, u32[]{:S(2)}, u32[]{:S(2)}) async-start(bf16[8,160,896]{2,0,1:T(8,128)(2,1)} %copy.143), calls=%async_computation | async-start | bytes 4587520 | tf_op jit(solution)/shard_map/all_to_all | solution.py:21
  51.3 1.4 copy-start.1
  62.4 1.9 %copy-start = (f32[2,10,128,384]{2,3,1,0:T(8,128)}, f32[2,10,128,384]{2,3,1,0:T(8,128)S(1)}, u32[]{:S(2)}) copy-start(f32[2,10,128,384]{2,3,1,0:T(8,128)S(1)} %convolution_bitcast_fusion) | copy-start | bytes 11796484
  62.4 1.9 %copy-start.11 = (bf16[2,8,128,128]{3,2,1,0:T(8,128)(2,1)S(1)}, bf16[2,8,128,128]{3,2,1,0:T(8,128)(2,1)}, u32[]{:S(2)}) copy-start(bf16[2,8,128,128]{3,2,1,0:T(8,128)(2,1)} %copy.218) | copy-start | bytes 1572868
  62.9 2.6 %copy-start.3 = (bf16[10,128,384]{1,2,0:T(8,128)(2,1)}, bf16[10,128,384]{1,2,0:T(8,128)(2,1)S(1)}, u32[]{:S(2)}) copy-start(bf16[10,128,384]{1,2,0:T(8,128)(2,1)S(1)} %fusion.1) | copy-start | bytes 2949124
  64.8 1.3 copy-start.29
  64.8 1.3 copy-start.31
  67.5 28.1 %all-to-all-start.1 = ((bf16[16,10,8,640]{3,2,1,0:T(8,128)(2,1)}), bf16[16,10,8,640]{3,2,1,0:T(8,128)(2,1)}, u32[]{:S(2)}, u32[]{:S(2)}) async-start(bf16[16,10,8,640]{3,2,1,0:T(8,128)(2,1)} %copy_bitcast_fusion.1), calls=%async_computation.1 | async-start | bytes 3276800 | tf_op jit(solution)/shard_map/all_to_all | solution.py:29
  95.6 3.4 %copy-start.7 = (bf16[2,8,40,160]{3,2,1,0:T(8,128)(2,1)S(1)}, bf16[2,8,40,160]{3,2,1,0:T(8,128)(2,1)}, u32[]{:S(2)}) copy-start(bf16[2,8,40,160]{3,2,1,0:T(8,128)(2,1)} %copy-done.6) | copy-start | bytes 614404
  96.6 5.6 %copy-start.18 = (bf16[1,320,128]{2,1,0:T(8,128)(2,1)S(1)}, bf16[1,320,128]{2,1,0:T(8,128)(2,1)}, u32[]{:S(2)}) copy-start(bf16[1,320,128]{2,1,0:T(8,128)(2,1)} %param.9) | copy-start | bytes 245764
  96.6 8.3 %copy-start.26 = (bf16[320,128]{1,0:T(8,128)(2,1)S(1)}, bf16[320,128]{1,0:T(8,128)(2,1)}, u32[]{:S(2)}) copy-start(bf16[320,128]{1,0:T(8,128)(2,1)} %param.13) | copy-start | bytes 245764
  99.0 9.8 %copy-start.9 = (bf16[160,8,2,128]{3,1,2,0:T(8,128)(2,1)}, bf16[160,8,2,128]{3,1,2,0:T(8,128)(2,1)S(1)}, u32[]{:S(2)}) copy-start(bf16[160,8,2,128]{3,1,2,0:T(8,128)(2,1)S(1)} %get-tuple-element.35) | copy-start | bytes 1966084
  99.0 9.4 %copy-start.19 = (bf16[320,128]{1,0:T(8,128)(2,1)S(1)}, bf16[320,128]{1,0:T(8,128)(2,1)}, u32[]{:S(2)}) copy-start(bf16[320,128]{1,0:T(8,128)(2,1)} %param.10) | copy-start | bytes 245764
  100.3 4.6 %collective-permute-start.1 = (bf16[8,40,128]{2,1,0:T(8,128)(2,1)S(1)}, bf16[8,40,128]{2,1,0:T(8,128)(2,1)S(1)}, u32[]{:S(2)}, u32[]{:S(2)}) collective-permute-start(bf16[8,40,128]{2,1,0:T(8,128)(2,1)S(1)} %fusion.35), channel_id=1, source_target_pairs={{16,0},{32,16},{48,32},{64,48},{80,64},{96,80},{112,96},{128,112},... | collective-permute-start | bytes 245768 | tf_op jit(solution)/shard_map/ppermute | solution.py:17
  102.6 5.8 %collective-permute-start = (bf16[8,40,128]{2,1,0:T(8,128)(2,1)S(1)}, bf16[8,40,128]{2,1,0:T(8,128)(2,1)S(1)}, u32[]{:S(2)}, u32[]{:S(2)}) collective-permute-start(bf16[8,40,128]{2,1,0:T(8,128)(2,1)S(1)} %fusion.36), channel_id=1, source_target_pairs={{0,16},{16,32},{32,48},{48,64},{64,80},{80,96},{96,112},{112,128},... | collective-permute-start | bytes 245768 | tf_op jit(solution)/shard_map/ppermute | solution.py:17
  105.0 3.3 %copy-start.23 = (bf16[8,40,128]{2,1,0:T(8,128)(2,1)}, bf16[8,40,128]{2,1,0:T(8,128)(2,1)S(1)}, u32[]{:S(2)}) copy-start(bf16[8,40,128]{2,1,0:T(8,128)(2,1)S(1)} %broadcast_select_fusion) | copy-start | bytes 245764
  108.3 0.6 copy-start.20
  109.4 20.7 %copy-start.12 = (bf16[2,8,128,128]{3,2,1,0:T(8,128)(2,1)S(1)}, bf16[2,8,128,128]{3,2,1,0:T(8,128)(2,1)}, u32[]{:S(2)}) copy-start(bf16[2,8,128,128]{3,2,1,0:T(8,128)(2,1)} %copy.218) | copy-start | bytes 1572868
  130.1 2.2 %copy-start.5 = (bf16[16,8,10,384]{3,1,0,2:T(8,128)(2,1)}, bf16[16,8,10,384]{3,1,0,2:T(8,128)(2,1)S(1)}, u32[]{:S(2)}) copy-start(bf16[16,8,10,384]{3,1,0,2:T(8,128)(2,1)S(1)} %copy.263) | copy-start | bytes 2949124
  132.3 1.0 copy-start.32
  132.3 1.6 copy-start.33
  137.0 1.5 copy-start.13
  138.5 1.0 copy-start.14
  138.5 1.1 copy-start.15
  140.7 7.2 %copy-start.10 = (bf16[160,8,2,128]{3,1,2,0:T(8,128)(2,1)S(1)}, bf16[160,8,2,128]{3,1,2,0:T(8,128)(2,1)}, u32[]{:S(2)}) copy-start(bf16[160,8,2,128]{3,1,2,0:T(8,128)(2,1)} %copy-done.9) | copy-start | bytes 1966084
  140.7 21.5 %all-to-all-start.3 = ((bf16[16,10,8,384]{3,2,1,0:T(8,128)(2,1)}), bf16[16,10,8,384]{3,2,1,0:T(8,128)(2,1)}, u32[]{:S(2)}, u32[]{:S(2)}) async-start(bf16[16,10,8,384]{3,2,1,0:T(8,128)(2,1)} %copy_bitcast_fusion.2), calls=%async_computation.3 | async-start | bytes 1966080 | tf_op jit(solution)/shard_map/all_to_all | solution.py:29
  146.0 2.9 %copy-start.24 = (bf16[8,40,128]{2,1,0:T(8,128)(2,1)S(1)}, bf16[8,40,128]{2,1,0:T(8,128)(2,1)}, u32[]{:S(2)}) copy-start(bf16[8,40,128]{2,1,0:T(8,128)(2,1)} %copy-done.23) | copy-start | bytes 245764
  146.0 2.9 %copy-start.28 = (bf16[1,320,128]{2,1,0:T(8,128)(2,1)S(1)}, bf16[1,320,128]{2,1,0:T(8,128)(2,1)}, u32[]{:S(2)}) copy-start(bf16[1,320,128]{2,1,0:T(8,128)(2,1)} %param.12) | copy-start | bytes 245764
  147.9 4.8 %copy-start.2 = (bf16[128,10,768]{0,2,1:T(8,128)(2,1)S(1)}, bf16[128,10,768]{0,2,1:T(8,128)(2,1)}, u32[]{:S(2)}) copy-start(bf16[128,10,768]{0,2,1:T(8,128)(2,1)} %copy.145) | copy-start | bytes 5898244
  148.9 3.8 %copy-start.30 = (bf16[1,10,128,128]{2,3,1,0:T(8,128)(2,1)S(1)}, bf16[1,10,128,128]{2,3,1,0:T(8,128)(2,1)}, u32[]{:S(2)}) copy-start(bf16[1,10,128,128]{2,3,1,0:T(8,128)(2,1)} %copy-done.29) | copy-start | bytes 983044
  154.4 1.3 copy-start.4
  154.4 1.5 copy-start.22
  155.9 8.6 %copy-start.8 = (bf16[2,8,40,160]{3,2,1,0:T(8,128)(2,1)S(1)}, bf16[2,8,40,160]{3,2,1,0:T(8,128)(2,1)}, u32[]{:S(2)}) copy-start(bf16[2,8,40,160]{3,2,1,0:T(8,128)(2,1)} %copy-done.6) | copy-start | bytes 614404
  155.9 8.6 %copy-start.25 = (bf16[8,40,128]{2,1,0:T(8,128)(2,1)S(1)}, bf16[8,40,128]{2,1,0:T(8,128)(2,1)}, u32[]{:S(2)}) copy-start(bf16[8,40,128]{2,1,0:T(8,128)(2,1)} %copy-done.23) | copy-start | bytes 245764
  163.2 2.4 %copy-start.16 = (bf16[160,8,2,128]{3,0,2,1:T(8,128)(2,1)S(1)}, bf16[160,8,2,128]{3,0,2,1:T(8,128)(2,1)}, u32[]{:S(2)}) copy-start(bf16[160,8,2,128]{3,0,2,1:T(8,128)(2,1)} %copy.160) | copy-start | bytes 1966084
  165.7 1.7 %copy-start.21 = (bf16[8,40,128]{2,1,0:T(8,128)(2,1)S(1)}, bf16[8,40,128]{2,1,0:T(8,128)(2,1)}, u32[]{:S(2)}) copy-start(bf16[8,40,128]{2,1,0:T(8,128)(2,1)} %copy-done.20) | copy-start | bytes 245764
where the time goes:
time: 169 us; the launch traced here: 168 us
  waiting for transfers between devices  63 us (37%)
  local copies, waits for them, and re-layouts  41.2 us (24%)
  blocking collectives  20.6 us (12%)
  starting transfers between devices  20.3 us (12%)
  matrix products  18.5 us (11%)
  other arithmetic  3.42 us (2%)
    all_to_all x1, waiting for transfers between devices, to_blocks(): lax.all_to_all(pieces, 'blk', split_axis=1, concat_axis=0, tiled=True)  31.3 us
    all_to_all x2, waiting for transfers between devices, to_features(): lax.all_to_all(grouped, 'blk', split_axis=0, concat_axis=0, tiled=True)  28.6 us
    all_to_all x1, blocking collectives, to_blocks(): lax.all_to_all(pieces, 'blk', split_axis=1, concat_axis=0, tiled=True)  20.6 us
    unnamed x74, local copies, waits for them, and re-layouts  10 us
    all_to_all x2, starting transfers between devices, to_features(): lax.all_to_all(grouped, 'blk', split_axis=0, concat_axis=0, tiled=True)  8.86 us
    all_to_all x1, starting transfers between devices, to_blocks(): lax.all_to_all(pieces, 'blk', split_axis=1, concat_axis=0, tiled=True)  7.16 us
    slice x2, local copies, waits for them, and re-layouts, shards(): arrived[:, :, :6 * t].reshape(FIRST_BLOCKS, hidden_blocks, 2, 3 * t)  5.45 us
    ppermute x2, starting transfers between devices, from_behind(): return lax.ppermute(value, axis, pairs)  4.33 us
  transfers between devices with their start and end apart: 5, of which 4 were waited for; matrix products, arithmetic and copies ran while one was open for 9% of the time, Pallas kernels for 0%

commit v1 on v0

--- a/solution.py
+++ b/solution.py
@@ -18,7 +18,10 @@
 
 
 def to_blocks(pieces):
-    return lax.all_to_all(pieces, "blk", split_axis=1, concat_axis=0, tiled=True)
+    return jnp.concatenate(
+        lax.all_to_all(jnp.stack(jnp.split(pieces, lax.axis_size("blk"), axis=1)), "blk", 0, 0),
+        axis=0,
+    )
 
 
 def to_features(pieces):

time: 169 us -> 170 us (level)
  the two profiles are of different devices: /device:TPU:224 before, /device:TPU:96 now
where the time goes in v1:
time: 170 us; the launch traced here: 169 us
  waiting for transfers between devices  64.8 us (38%)
  local copies, waits for them, and re-layouts  38.2 us (22%)
  blocking collectives  20.5 us (12%)
  starting transfers between devices  20.4 us (12%)
  matrix products  18.5 us (11%)
  other arithmetic  4.74 us (3%)
    all_to_all x1, waiting for transfers between devices, to_blocks(): lax.all_to_all(jnp.stack(jnp.split(pieces, lax.axis_size('blk'), axis=1))...  33.2 us
    all_to_all x2, waiting for transfers between devices, to_features(): lax.all_to_all(grouped, 'blk', split_axis=0, concat_axis=0, tiled=True)  28.5 us
    all_to_all x1, blocking collectives, to_blocks(): lax.all_to_all(jnp.stack(jnp.split(pieces, lax.axis_size('blk'), axis=1))...  20.5 us
    unnamed x74, local copies, waits for them, and re-layouts  9.16 us
    all_to_all x2, starting transfers between devices, to_features(): lax.all_to_all(grouped, 'blk', split_axis=0, concat_axis=0, tiled=True)  8.86 us
    all_to_all x1, starting transfers between devices, to_blocks(): lax.all_to_all(jnp.stack(jnp.split(pieces, lax.axis_size('blk'), axis=1))...  7.21 us
    slice x2, local copies, waits for them, and re-layouts, shards(): arrived[:, :, :6 * t].reshape(FIRST_BLOCKS, hidden_blocks, 2, 3 * t)  5.45 us
    ppermute x2, starting transfers between devices, from_behind(): return lax.ppermute(value, axis, pairs)  4.33 us
  transfers between devices with their start and end apart: 5, of which 4 were waited for; matrix products, arithmetic and copies ran while one was open for 8% of the time, Pallas kernels for 0%

profile of v1, /device:TPU:96, one launch (start us, length us, event | category | flops | bytes accessed | tf_op | source)
XLA Modules:
  0.0 168.5 jit_solution(14393300950917367145)
XLA Ops:
  0.6 0.9 fusion.137
  1.6 1.4 reshape_squeeze.27
  3.0 1.6 reshape_squeeze.28
  4.5 1.6 convert_bitcast_fusion
  6.4 0.7 copy-done.27
  8.4 1.9 %copy.181 = bf16[16,8,10,896]{3,1,2,0:T(8,128)(2,1)} copy(bf16[16,8,10,896]{3,2,1,0:T(8,128)(2,1)S(1)} %fusion.88) | data formatting | bytes 4587520 | tf_op jit(solution)/shard_map/stack | solution.py:22
  10.3 7.2 %all-to-all-start = ((bf16[16,8,10,896]{3,1,2,0:T(8,128)(2,1)}), bf16[16,8,10,896]{3,1,2,0:T(8,128)(2,1)}, u32[]{:S(2)}, u32[]{:S(2)}) async-start(bf16[16,8,10,896]{3,1,2,0:T(8,128)(2,1)} %copy.181), calls=%async_computation | async-start | bytes 4587520 | tf_op jit(solution)/shard_map/all_to_all | solution.py:22
  17.5 0.9 copy.260
  18.9 33.2 %all-to-all-done = bf16[16,8,10,896]{3,1,2,0:T(8,128)(2,1)} async-done(((bf16[16,8,10,896]{3,1,2,0:T(8,128)(2,1)}), bf16[16,8,10,896]{3,1,2,0:T(8,128)(2,1)}, u32[]{:S(2)}, u32[]{:S(2)}) %all-to-all-start) | async-done | bytes 2293792 | tf_op jit(solution)/shard_map/all_to_all | solution.py:22
  52.1 2.0 %copy.304 = bf16[16,8,10,896]{3,1,0,2:T(8,128)(2,1)S(1)} copy(bf16[16,8,10,896]{3,1,2,0:T(8,128)(2,1)} %all-to-all-done) | data formatting | bytes 4587520 | tf_op jit(solution)/shard_map/all_to_all | solution.py:22
  54.1 1.5 slice.113
  55.5 4.0 %copy.183 = bf16[128,10,768]{0,2,1:T(8,128)(2,1)} copy(bf16[128,10,768]{2,0,1:T(8,128)(2,1)} %slice.113) | data formatting | bytes 3932160 | tf_op jit(solution)/shard_map/slice | solution.py:115
  59.5 2.2 %convolution_bitcast_fusion = f32[2,10,128,384]{2,3,1,0:T(8,128)S(1)} fusion(bf16[128,10,2,384]{0,3,2,1:T(8,128)(2,1)} %bitcast.307, bf16[2,10,128,128]{3,2,0,1:T(8,128)(2,1)S(1)} %reshape_squeeze.30), kind=kOutput, calls=%fused_computation.31 | convolution fusion | flops 251658240 | bytes 6553600 | tf_op jit(solution)/shard_map/prgt,grpo->grot/dot_general | solution.py:49
  62.3 1.3 copy-done
  64.2 0.6 fusion.17
  65.4 1.4 copy_bitcast_fusion.1
  66.8 4.4 %all-to-all-start.1 = ((bf16[16,10,8,640]{3,2,1,0:T(8,128)(2,1)}), bf16[16,10,8,640]{3,2,1,0:T(8,128)(2,1)}, u32[]{:S(2)}, u32[]{:S(2)}) async-start(bf16[16,10,8,640]{3,2,1,0:T(8,128)(2,1)} %copy_bitcast_fusion.1), calls=%async_computation.1 | async-start | bytes 3276800 | tf_op jit(solution)/shard_map/all_to_all | solution.py:32
  71.3 23.6 %all-to-all-done.1 = bf16[16,10,8,640]{3,2,1,0:T(8,128)(2,1)} async-done(((bf16[16,10,8,640]{3,2,1,0:T(8,128)(2,1)}), bf16[16,10,8,640]{3,2,1,0:T(8,128)(2,1)}, u32[]{:S(2)}, u32[]{:S(2)}) %all-to-all-start.1) | async-done | bytes 1638432 | tf_op jit(solution)/shard_map/all_to_all | solution.py:32
  94.9 1.0 slice.121
  96.0 2.3 %fusion.136 = (bf16[160,8,256]{2,1,0:T(8,128)(2,1)}, bf16[160,8,2,128]{3,1,2,0:T(8,128)(2,1)S(1)}) fusion(bf16[160,8,640]{2,1,0:T(8,128)(2,1)} %bitcast.40), kind=kLoop, calls=%fused_computation.267 | loop fusion | bytes 2621440 | tf_op jit(solution)/shard_map/slice | solution.py:157
  98.3 1.4 fusion.35
  99.7 1.9 %collective-permute-start.1 = (bf16[8,40,128]{2,1,0:T(8,128)(2,1)S(1)}, bf16[8,40,128]{2,1,0:T(8,128)(2,1)S(1)}, u32[]{:S(2)}, u32[]{:S(2)}) collective-permute-start(bf16[8,40,128]{2,1,0:T(8,128)(2,1)S(1)} %fusion.35), channel_id=1, source_target_pairs={{16,0},{32,16},{48,32},{64,48},{80,64},{96,80},{112,96},{128,112},... | collective-permute-start | bytes 245768 | tf_op jit(solution)/shard_map/ppermute | solution.py:17
  101.9 2.4 %collective-permute-start = (bf16[8,40,128]{2,1,0:T(8,128)(2,1)S(1)}, bf16[8,40,128]{2,1,0:T(8,128)(2,1)S(1)}, u32[]{:S(2)}, u32[]{:S(2)}) collective-permute-start(bf16[8,40,128]{2,1,0:T(8,128)(2,1)S(1)} %fusion.36), channel_id=1, source_target_pairs={{0,16},{16,32},{32,48},{48,64},{64,80},{80,96},{96,112},{112,128},... | collective-permute-start | bytes 245768 | tf_op jit(solution)/shard_map/ppermute | solution.py:17
  104.6 3.1 %collective-permute-done = bf16[8,40,128]{2,1,0:T(8,128)(2,1)S(1)} collective-permute-done((bf16[8,40,128]{2,1,0:T(8,128)(2,1)S(1)}, bf16[8,40,128]{2,1,0:T(8,128)(2,1)S(1)}, u32[]{:S(2)}, u32[]{:S(2)}) %collective-permute-start) | collective-permute-done | bytes 81952 | tf_op jit(solution)/shard_map/ppermute | solution.py:17
  107.6 0.6 copy-done.20
  109.7 20.5 %all_to_all.20 = bf16[16,8,10,384]{3,1,2,0:T(8,128)(2,1)S(1)} all-to-all(bf16[16,8,10,384]{3,1,2,0:T(8,128)(2,1)S(1)} %copy.203), channel_id=1, replica_groups=mesh['section'=32,'blk'=16] {'blk'}, dimensions={0} | all-to-all | bytes 1966080 | tf_op jit(solution)/shard_map/all_to_all | solution.py:22
  130.3 2.2 %fusion.67 = (bf16[1,10,128,128]{2,3,1,0:T(8,128)(2,1)S(1)}, bf16[1,10,128,128]{2,3,1,0:T(8,128)(2,1)S(1)}) fusion(f32[2,10,128,384]{2,3,1,0:T(8,128)} %copy-done, bf16[16,128,128]{2,1,0:T(8,128)(2,1)S(1)} %bitcast.315, bf16[128,10,384]{2,0,1:T(8,128)(2,1)S(1)} %bitcast.309), kind=kOutput, calls=%fused_computation.164 | convolution fusion | flops 44072960 | bytes 2621440 | tf_op jit(solution)/shard_map/prt,rop->rot/dot_general | solution.py:58
  132.5 1.0 slice.123
  134.1 0.9 slice_bitcast_fusion.11
  135.0 2.2 %copy.205 = bf16[128,10,256]{0,2,1:T(8,128)(2,1)} copy(bf16[128,10,256]{2,0,1:T(8,128)(2,1)} %slice.123) | data formatting | bytes 1310720 | tf_op jit(solution)/shard_map/slice | solution.py:141
  137.3 1.5 convolution_bitcast_fusion.1
  139.8 1.2 copy_bitcast_fusion.2
  141.0 4.4 %all-to-all-start.3 = ((bf16[16,10,8,384]{3,2,1,0:T(8,128)(2,1)}), bf16[16,10,8,384]{3,2,1,0:T(8,128)(2,1)}, u32[]{:S(2)}, u32[]{:S(2)}) async-start(bf16[16,10,8,384]{3,2,1,0:T(8,128)(2,1)} %copy_bitcast_fusion.2), calls=%async_computation.3 | async-start | bytes 1966080 | tf_op jit(solution)/shard_map/all_to_all | solution.py:32
  145.4 0.8 slice.116
  146.2 1.9 %copy.252 = bf16[128,10,128]{0,2,1:T(8,128)(2,1)} copy(bf16[128,10,128]{2,0,1:T(8,128)(2,1)} %slice.116) | data formatting | bytes 655360
  148.2 1.0 copy.198
  149.2 1.4 fusion.32
  150.9 1.1 reshape.95
  151.9 1.0 slice.126
  152.9 1.7 %fusion.3 = bf16[2,10,128,128]{3,2,1,0:T(8,128)(2,1)S(1)} fusion(bf16[1,10,128,128]{2,3,1,0:T(8,128)(2,1)} %copy-done.33, bf16[1,10,128,128]{2,3,1,0:T(8,128)(2,1)} %copy-done.32, bf16[1,10,128,128]{2,3,1,0:T(8,128)(2,1)} %copy-done.31, bf16[1,10,128,128]{2,3,1,0:T(8,128)(2,1)S(1)} %copy-done.30, bf16[128,10,2,384]{0,3,2,1:T(8,128)(2,1)S(1)} %bitcast.308), kind=kOutput, calls=%fused_computation.58 | convolution fusion | flops 173670400 | bytes 3276800 | tf_op jit(solution)/shard_map/prgt,grot->grpo/dot_general | solution.py:162
  154.7 1.0 reshape.93
  156.6 1.0 reshape.94
  157.6 4.9 %all-to-all-done.3 = bf16[16,10,8,384]{3,2,1,0:T(8,128)(2,1)} async-done(((bf16[16,10,8,384]{3,2,1,0:T(8,128)(2,1)}), bf16[16,10,8,384]{3,2,1,0:T(8,128)(2,1)}, u32[]{:S(2)}, u32[]{:S(2)}) %all-to-all-start.3) | async-done | bytes 983072 | tf_op jit(solution)/shard_map/all_to_all | solution.py:32
  162.5 1.0 slice.131
  163.5 1.3 slice_bitcast_fusion.2
  164.8 1.0 add_convert_fusion
  166.9 0.7 copy.229
  167.6 0.9 add_convert_fusion.1
  (121 shorter events, 9.6 us)
Async XLA Ops:
  2.9 1.6 copy-start.5
  6.2 0.9 copy-start.27
  10.3 7.2 %copy-start.17 = (bf16[1,10,16384]{2,1,0:T(8,128)(2,1)S(1)}, bf16[1,10,16384]{2,1,0:T(8,128)(2,1)}, u32[]{:S(2)}) copy-start(bf16[1,10,16384]{2,1,0:T(8,128)(2,1)} %param.16) | copy-start | bytes 983044
  10.3 8.1 %copy-start.15 = (bf16[1,2,10,16384]{3,1,2,0:T(2,128)(2,1)S(1)}, bf16[1,2,10,16384]{3,1,2,0:T(2,128)(2,1)}, u32[]{:S(2)}) copy-start(bf16[1,2,10,16384]{3,1,2,0:T(2,128)(2,1)} %param.15) | copy-start | bytes 1966084
  10.3 41.8 %all-to-all-start = ((bf16[16,8,10,896]{3,1,2,0:T(8,128)(2,1)}), bf16[16,8,10,896]{3,1,2,0:T(8,128)(2,1)}, u32[]{:S(2)}, u32[]{:S(2)}) async-start(bf16[16,8,10,896]{3,1,2,0:T(8,128)(2,1)} %copy.181), calls=%async_computation | async-start | bytes 4587520 | tf_op jit(solution)/shard_map/all_to_all | solution.py:22
  61.7 1.9 %copy-start = (f32[2,10,128,384]{2,3,1,0:T(8,128)}, f32[2,10,128,384]{2,3,1,0:T(8,128)S(1)}, u32[]{:S(2)}) copy-start(f32[2,10,128,384]{2,3,1,0:T(8,128)S(1)} %convolution_bitcast_fusion) | copy-start | bytes 11796484
  61.7 1.9 %copy-start.10 = (bf16[2,8,128,128]{3,2,1,0:T(8,128)(2,1)S(1)}, bf16[2,8,128,128]{3,2,1,0:T(8,128)(2,1)}, u32[]{:S(2)}) copy-start(bf16[2,8,128,128]{3,2,1,0:T(8,128)(2,1)} %copy.260) | copy-start | bytes 1572868
  62.3 2.5 %copy-start.2 = (bf16[10,128,384]{1,2,0:T(8,128)(2,1)}, bf16[10,128,384]{1,2,0:T(8,128)(2,1)S(1)}, u32[]{:S(2)}) copy-start(bf16[10,128,384]{1,2,0:T(8,128)(2,1)S(1)} %fusion.1) | copy-start | bytes 2949124
  64.1 1.2 copy-start.29
  64.2 1.2 copy-start.31
  66.8 28.1 %all-to-all-start.1 = ((bf16[16,10,8,640]{3,2,1,0:T(8,128)(2,1)}), bf16[16,10,8,640]{3,2,1,0:T(8,128)(2,1)}, u32[]{:S(2)}, u32[]{:S(2)}) async-start(bf16[16,10,8,640]{3,2,1,0:T(8,128)(2,1)} %copy_bitcast_fusion.1), calls=%async_computation.1 | async-start | bytes 3276800 | tf_op jit(solution)/shard_map/all_to_all | solution.py:32
  94.9 3.4 %copy-start.6 = (bf16[2,8,40,160]{3,2,1,0:T(8,128)(2,1)S(1)}, bf16[2,8,40,160]{3,2,1,0:T(8,128)(2,1)}, u32[]{:S(2)}) copy-start(bf16[2,8,40,160]{3,2,1,0:T(8,128)(2,1)} %copy-done.5) | copy-start | bytes 614404
  96.0 5.6 %copy-start.18 = (bf16[1,320,128]{2,1,0:T(8,128)(2,1)S(1)}, bf16[1,320,128]{2,1,0:T(8,128)(2,1)}, u32[]{:S(2)}) copy-start(bf16[1,320,128]{2,1,0:T(8,128)(2,1)} %param.9) | copy-start | bytes 245764
  96.0 8.3 %copy-start.26 = (bf16[320,128]{1,0:T(8,128)(2,1)S(1)}, bf16[320,128]{1,0:T(8,128)(2,1)}, u32[]{:S(2)}) copy-start(bf16[320,128]{1,0:T(8,128)(2,1)} %param.13) | copy-start | bytes 245764
  98.3 10.4 %copy-start.8 = (bf16[160,8,2,128]{3,1,2,0:T(8,128)(2,1)}, bf16[160,8,2,128]{3,1,2,0:T(8,128)(2,1)S(1)}, u32[]{:S(2)}) copy-start(bf16[160,8,2,128]{3,1,2,0:T(8,128)(2,1)S(1)} %get-tuple-element.35) | copy-start | bytes 1966084
  98.3 10.0 %copy-start.19 = (bf16[320,128]{1,0:T(8,128)(2,1)S(1)}, bf16[320,128]{1,0:T(8,128)(2,1)}, u32[]{:S(2)}) copy-start(bf16[320,128]{1,0:T(8,128)(2,1)} %param.10) | copy-start | bytes 245764
  99.7 4.6 %collective-permute-start.1 = (bf16[8,40,128]{2,1,0:T(8,128)(2,1)S(1)}, bf16[8,40,128]{2,1,0:T(8,128)(2,1)S(1)}, u32[]{:S(2)}, u32[]{:S(2)}) collective-permute-start(bf16[8,40,128]{2,1,0:T(8,128)(2,1)S(1)} %fusion.35), channel_id=1, source_target_pairs={{16,0},{32,16},{48,32},{64,48},{80,64},{96,80},{112,96},{128,112},... | collective-permute-start | bytes 245768 | tf_op jit(solution)/shard_map/ppermute | solution.py:17
  101.9 5.8 %collective-permute-start = (bf16[8,40,128]{2,1,0:T(8,128)(2,1)S(1)}, bf16[8,40,128]{2,1,0:T(8,128)(2,1)S(1)}, u32[]{:S(2)}, u32[]{:S(2)}) collective-permute-start(bf16[8,40,128]{2,1,0:T(8,128)(2,1)S(1)} %fusion.36), channel_id=1, source_target_pairs={{0,16},{16,32},{32,48},{48,64},{64,80},{80,96},{96,112},{112,128},... | collective-permute-start | bytes 245768 | tf_op jit(solution)/shard_map/ppermute | solution.py:17
  104.3 3.3 %copy-start.23 = (bf16[8,40,128]{2,1,0:T(8,128)(2,1)}, bf16[8,40,128]{2,1,0:T(8,128)(2,1)S(1)}, u32[]{:S(2)}) copy-start(bf16[8,40,128]{2,1,0:T(8,128)(2,1)S(1)} %broadcast_select_fusion) | copy-start | bytes 245764
  107.6 0.6 copy-start.20
  109.7 20.7 %copy-start.11 = (bf16[2,8,128,128]{3,2,1,0:T(8,128)(2,1)S(1)}, bf16[2,8,128,128]{3,2,1,0:T(8,128)(2,1)}, u32[]{:S(2)}) copy-start(bf16[2,8,128,128]{3,2,1,0:T(8,128)(2,1)} %copy.260) | copy-start | bytes 1572868
  130.3 2.2 %copy-start.4 = (bf16[16,8,10,384]{3,1,0,2:T(8,128)(2,1)}, bf16[16,8,10,384]{3,1,0,2:T(8,128)(2,1)S(1)}, u32[]{:S(2)}) copy-start(bf16[16,8,10,384]{3,1,0,2:T(8,128)(2,1)S(1)} %copy.305) | copy-start | bytes 2949124
  132.5 1.0 copy-start.32
  132.5 1.6 copy-start.33
  137.3 1.5 copy-start.12
  138.7 1.0 copy-start.13
  138.8 1.1 copy-start.14
  141.0 7.2 %copy-start.9 = (bf16[160,8,2,128]{3,1,2,0:T(8,128)(2,1)S(1)}, bf16[160,8,2,128]{3,1,2,0:T(8,128)(2,1)}, u32[]{:S(2)}) copy-start(bf16[160,8,2,128]{3,1,2,0:T(8,128)(2,1)} %copy-done.8) | copy-start | bytes 1966084
  141.0 21.5 %all-to-all-start.3 = ((bf16[16,10,8,384]{3,2,1,0:T(8,128)(2,1)}), bf16[16,10,8,384]{3,2,1,0:T(8,128)(2,1)}, u32[]{:S(2)}, u32[]{:S(2)}) async-start(bf16[16,10,8,384]{3,2,1,0:T(8,128)(2,1)} %copy_bitcast_fusion.2), calls=%async_computation.3 | async-start | bytes 1966080 | tf_op jit(solution)/shard_map/all_to_all | solution.py:32
  146.2 2.9 %copy-start.24 = (bf16[8,40,128]{2,1,0:T(8,128)(2,1)S(1)}, bf16[8,40,128]{2,1,0:T(8,128)(2,1)}, u32[]{:S(2)}) copy-start(bf16[8,40,128]{2,1,0:T(8,128)(2,1)} %copy-done.23) | copy-start | bytes 245764
  146.2 2.9 %copy-start.28 = (bf16[1,320,128]{2,1,0:T(8,128)(2,1)S(1)}, bf16[1,320,128]{2,1,0:T(8,128)(2,1)}, u32[]{:S(2)}) copy-start(bf16[1,320,128]{2,1,0:T(8,128)(2,1)} %param.12) | copy-start | bytes 245764
  148.2 4.8 %copy-start.1 = (bf16[128,10,768]{0,2,1:T(8,128)(2,1)S(1)}, bf16[128,10,768]{0,2,1:T(8,128)(2,1)}, u32[]{:S(2)}) copy-start(bf16[128,10,768]{0,2,1:T(8,128)(2,1)} %copy.183) | copy-start | bytes 5898244
  149.2 3.8 %copy-start.30 = (bf16[1,10,128,128]{2,3,1,0:T(8,128)(2,1)S(1)}, bf16[1,10,128,128]{2,3,1,0:T(8,128)(2,1)}, u32[]{:S(2)}) copy-start(bf16[1,10,128,128]{2,3,1,0:T(8,128)(2,1)} %copy-done.29) | copy-start | bytes 983044
  154.7 1.3 copy-start.3
  154.7 1.5 copy-start.22
  156.2 8.6 %copy-start.7 = (bf16[2,8,40,160]{3,2,1,0:T(8,128)(2,1)S(1)}, bf16[2,8,40,160]{3,2,1,0:T(8,128)(2,1)}, u32[]{:S(2)}) copy-start(bf16[2,8,40,160]{3,2,1,0:T(8,128)(2,1)} %copy-done.5) | copy-start | bytes 614404
  156.2 8.6 %copy-start.25 = (bf16[8,40,128]{2,1,0:T(8,128)(2,1)S(1)}, bf16[8,40,128]{2,1,0:T(8,128)(2,1)}, u32[]{:S(2)}) copy-start(bf16[8,40,128]{2,1,0:T(8,128)(2,1)} %copy-done.23) | copy-start | bytes 245764
  163.5 2.4 %copy-start.16 = (bf16[160,8,2,128]{3,0,2,1:T(8,128)(2,1)S(1)}, bf16[160,8,2,128]{3,0,2,1:T(8,128)(2,1)}, u32[]{:S(2)}) copy-start(bf16[160,8,2,128]{3,0,2,1:T(8,128)(2,1)} %copy.198) | copy-start | bytes 1966084
  165.9 1.7 %copy-start.21 = (bf16[8,40,128]{2,1,0:T(8,128)(2,1)S(1)}, bf16[8,40,128]{2,1,0:T(8,128)(2,1)}, u32[]{:S(2)}) copy-start(bf16[8,40,128]{2,1,0:T(8,128)(2,1)} %copy-done.20) | copy-start | bytes 245764
